TPU v7x, 32 devices: a whole 2x2x4 slice. The times are simulated.
32 devices in a mesh: groups: 2 (over y), section: 4 (over x, core), filt: 4 (over z).
Axes of the slice: x: 2, y: 2, z: 4, core: 2. Of those that a mesh axis runs over, the one named last changes fastest.
Arguments:
- volumes: bfloat16 [16, 256, 4, 2, 128], P('groups', 'filt'), parts along dimension 0, may hold values from -6 to 6
- weights: bfloat16 [4, 256, 27, 256], P('section', 'filt'), may hold values from -0.125 to 0.125
- biases: float32 [4, 256], P('section', 'filt'), may hold values from -3 to 3
- cotangent: bfloat16 [16, 256, 4, 2, 128], P('groups', 'filt'), parts along dimension 0, may hold values from -6 to 6
Outputs:
- grad_weights: float32 [8, 256, 27, 256], P(('groups', 'section'), 'filt'), parts along dimension 0
- grad_biases: float32 [8, 256], P(('groups', 'section'), 'filt'), parts along dimension 0
- grad_inputs: bfloat16 [8, 8, 256, 4, 2, 128], P(('groups', 'section'), None, 'filt'), parts along dimension 0
There are 2 independent parts, one for each index of `groups`. A program takes and returns all parts, laid end to end along the dimension named above; an argument that names none is the same for every part. Nothing has to cross between parts.
All inputs are finite; a program needn't handle non-finite values.
Results may differ from a plain program's by a relative error of at most 0.019.
Values may be sent and summed in bfloat16 or wider, within the bound.
No kernel may reach another device: no remote copies, remote signals or barrier semaphores. Data moves between devices by JAX's collectives and lax.ppermute only.
A program may use at most 64 MiB of HBM per device.

v0:
```python
import math
import jax
import jax.numpy as jnp
import numpy as np
from jax import lax
from jax.sharding import PartitionSpec as P

tap_offsets = [
    (first, second, third) for first in (-1, 0, 1) for second in (-1, 0, 1) for third in (-1, 0, 1)
]


def passed_along(value, axis, steps):
    count = lax.axis_size(axis)
    first, last = (max(0, -steps), min(count, count - steps))
    return lax.ppermute(value, axis, [(source, source + steps) for source in range(first, last)])


def for_sending(x):
    return jax.tree.map(lambda a: a.astype(jnp.bfloat16) if a.dtype == jnp.float32 else a, x)


def lane_shift(values, step):
    if step == 0:
        return values
    width = values.shape[-1]
    source = jnp.arange(width)[:, None]
    target = jnp.arange(width)[None, :]
    if values.dtype == jnp.float32:
        matrix = (source == target + step).astype(jnp.float32)
        return jnp.einsum(
            "...z,zw->...w",
            values,
            matrix,
            precision=lax.Precision.HIGHEST,
            preferred_element_type=jnp.float32,
        )
    matrix = (source == target + step).astype(values.dtype)
    return jnp.einsum("...z,zw->...w", values, matrix, preferred_element_type=jnp.float32).astype(
        values.dtype
    )


def row_shift(values, step_x, step_y, extent_x, extent_y):
    if step_x == 0 and step_y == 0:
        return values
    row_total = extent_x * extent_y
    delta = step_x * extent_y + step_y
    keep_mask = np.zeros((row_total, 1), dtype=bool)
    for row_pos in range(row_total):
        pos_x = row_pos // extent_y + step_x
        pos_y = row_pos % extent_y + step_y
        keep_mask[row_pos, 0] = 0 <= pos_x < extent_x and 0 <= pos_y < extent_y
    margin = extent_y + 1
    padded = jnp.pad(values, [(0, 0)] * (values.ndim - 2) + [(margin, margin), (0, 0)])
    sliced = lax.slice_in_dim(
        padded, margin + delta, margin + delta + row_total, axis=values.ndim - 2
    )
    return jnp.where(jnp.asarray(keep_mask), sliced, jnp.zeros((), values.dtype))


def sum_taps(product, direction, extent_x, extent_y):
    summed = jnp.zeros(product.shape[:1] + product.shape[2:], jnp.float32)
    for lane_step in (-1, 0, 1):
        partial_sum = jnp.zeros(product.shape[:1] + product.shape[2:], jnp.float32)
        for tap_index, offset in enumerate(tap_offsets):
            if offset[2] == lane_step:
                partial_sum = partial_sum + row_shift(
                    product[:, tap_index],
                    direction * offset[0],
                    direction * offset[1],
                    extent_x,
                    extent_y,
                )
        summed = summed + lane_shift(partial_sum, direction * lane_step)
    return summed


def stack_taps(values, direction, extent_x, extent_y):
    shifted_lanes = {}
    for lane_step in (-1, 0, 1):
        shifted_lanes[lane_step] = lane_shift(values, direction * lane_step)
    return jnp.stack(
        [
            row_shift(
                shifted_lanes[offset[2]],
                direction * offset[0],
                direction * offset[1],
                extent_x,
                extent_y,
            )
            for offset in tap_offsets
        ],
        axis=1,
    )


def silu_slope(pre_act):
    sigmoid = jax.nn.sigmoid(pre_act)
    return sigmoid * (1.0 + pre_act * (1.0 - sigmoid))


def store_slot(buffer, entry, position, in_range):
    previous = lax.dynamic_index_in_dim(buffer, position, 0, keepdims=False)
    return lax.dynamic_update_index_in_dim(
        buffer, jnp.where(in_range, entry, previous), position, 0
    )


def local(volumes, weights, biases, cotangent):
    section_count = lax.axis_size("section")
    section_pos = lax.axis_index("section")
    micro_count = volumes.shape[0]
    tick_count = micro_count + section_count - 1
    weight = weights[0]
    own_count, tap_count, channels = weight.shape
    weight_rows = weight.reshape(own_count * tap_count, channels)
    layer_bias = biases[0]
    extent_x, extent_y, lane_count = volumes.shape[2:]
    row_total = extent_x * extent_y
    cell_count = row_total * lane_count
    flat_volumes = volumes.reshape(micro_count, own_count, row_total, lane_count)
    flat_cotangent = cotangent.reshape(micro_count, own_count, row_total, lane_count)
    stored = jnp.zeros((micro_count, own_count, row_total, lane_count), jnp.bfloat16)
    saved_pre = jnp.zeros((micro_count, own_count, row_total, lane_count), jnp.float32)
    empty_slab = jnp.zeros((own_count, row_total, lane_count), jnp.bfloat16)

    def forward_tick(tick_now, carried):
        incoming, saved_pre, stored = carried
        sample = tick_now - section_pos
        in_range = (sample >= 0) & (sample < micro_count)
        position = jnp.clip(sample, 0, micro_count - 1)
        first_input = lax.dynamic_index_in_dim(flat_volumes, position, 0, keepdims=False)
        own_input = jnp.where(section_pos == 0, first_input, incoming)
        panel_part = jax.tree.map(
            lambda a: lax.all_gather(a, "filt", axis=0, tiled=True), own_input
        )
        columns = lax.slice_in_dim(weight_rows, 0, panel_part.shape[0], axis=1)
        product = jnp.zeros(
            (own_count * tap_count, row_total, lane_count), jnp.float32
        ) + jnp.einsum("ki,irz->krz", columns, panel_part, preferred_element_type=jnp.float32)
        stored = store_slot(stored, own_input, position, in_range)
        pre_act = (
            sum_taps(
                product.reshape(own_count, tap_count, row_total, lane_count), 1, extent_x, extent_y
            )
            + layer_bias[:, None, None]
        )
        saved_pre = store_slot(saved_pre, pre_act, position, in_range)
        outgoing = jax.nn.silu(pre_act).astype(jnp.bfloat16)
        incoming = passed_along(outgoing, "section", 1)
        return (incoming, saved_pre, stored)

    unused_slab, saved_pre, stored = lax.fori_loop(
        0, tick_count, forward_tick, (empty_slab, saved_pre, stored)
    )

    def backward_tick(tick_now, carried):
        incoming, grad_rows, grad_bias, grad_in = carried
        sample = tick_now - (section_count - 1 - section_pos)
        in_range = (sample >= 0) & (sample < micro_count)
        position = jnp.clip(sample, 0, micro_count - 1)
        last_grad = lax.dynamic_index_in_dim(flat_cotangent, position, 0, keepdims=False)
        upstream = jnp.where(section_pos == section_count - 1, last_grad, incoming)
        pre_act = lax.dynamic_index_in_dim(saved_pre, position, 0, keepdims=False)
        slope_grad = (upstream.astype(jnp.float32) * silu_slope(pre_act)).astype(jnp.bfloat16)
        stacked = stack_taps(slope_grad, -1, extent_x, extent_y).reshape(
            own_count * tap_count, row_total, lane_count
        )
        own_input = lax.dynamic_index_in_dim(stored, position, 0, keepdims=False)
        weight_term = jnp.einsum(
            "krz,irz->ki",
            stacked,
            lax.all_gather(for_sending(own_input), "filt", axis=0, tiled=True),
            preferred_element_type=jnp.float32,
        )
        grad_rows = grad_rows + jnp.where(in_range, weight_term, 0.0)
        grad_bias = grad_bias + jnp.where(
            in_range, jnp.sum(slope_grad.astype(jnp.float32), axis=(1, 2)), 0.0
        )
        columns = lax.slice_in_dim(weight_rows, 0, own_count * lax.axis_size("filt"), axis=1)
        input_grad = lax.psum_scatter(
            jnp.einsum("ki,krz->irz", columns, stacked, preferred_element_type=jnp.float32).astype(
                jnp.bfloat16
            ),
            "filt",
            scatter_dimension=0,
            tiled=True,
        ).astype(jnp.float32)
        input_grad = input_grad.astype(jnp.bfloat16)
        grad_in = store_slot(grad_in, input_grad, position, in_range)
        incoming = passed_along(input_grad, "section", -1)
        return (incoming, grad_rows, grad_bias, grad_in)

    start_state = (
        empty_slab,
        jnp.zeros((own_count * tap_count, channels), jnp.float32),
        jnp.zeros((own_count,), jnp.float32),
        jnp.zeros((micro_count, own_count, row_total, lane_count), jnp.bfloat16),
    )
    unused_grad, grad_rows, grad_bias, grad_in = lax.fori_loop(
        0, tick_count, backward_tick, start_state
    )
    norm_scale = 1.0 / math.sqrt(micro_count * cell_count)
    grad_out = grad_in.reshape(1, micro_count, own_count, extent_x, extent_y, lane_count)
    return (
        (grad_rows * norm_scale).reshape(1, own_count, tap_count, channels),
        (grad_bias * norm_scale)[None],
        grad_out,
    )


def solution(mesh):
    in_specs = (
        P("groups", "filt", None, None, None),
        P("section", "filt", None, None),
        P("section", "filt"),
        P("groups", "filt", None, None, None),
    )
    out_specs = (
        P(("groups", "section"), "filt", None, None),
        P(("groups", "section"), "filt"),
        P(("groups", "section"), None, "filt", None, None, None),
    )
    return jax.shard_map(local, mesh=mesh, in_specs=in_specs, out_specs=out_specs, check_vma=False)
```

profile of v0, /device:TPU:1, one launch (start us, length us, event | category | flops | bytes accessed | tf_op | source)
XLA Modules:
  0.0 1059.6 jit_solution(5570250423504639003)
XLA Ops:
  13.4 434.8 %while.45 = (s32[]{:T(128)}, bf16[64,8,128]{2,0,1:T(8,128)(2,1)S(1)}, f32[8,64,8,128]{3,1,2,0:T(8,128)}, bf16[8,64,8,128]{3,1,2,0:T(8,128)(2,1)}, pred[]{:T(512)...) while((s32[]{:T(128)}, ...), condition=%wide.region_1.2_spmd.clone.clone, body=%wide.region_0.1_spmd.sunk.clone.clone.sunk | while | flops 1111195904 | bytes 60796016 | solution.py:154
  15.1 15.3 %all_gather.26 = bf16[256,8,128]{2,0,1:T(8,128)(2,1)S(1)} all-gather(bf16[64,8,128]{2,0,1:T(8,128)(2,1)S(1)} %get-tuple-element.2151), channel_id=1, replica_groups=mesh['groups'=2,'section'=4,'filt'=4] {'filt'}, dimensions={0}, use_global_device_ids=true | all-gather | bytes 655360 | tf_op jit(solution)/shard_map/while/body/eval_jaxpr/all_gather | solution.py:136
  32.7 9.4 copy.273
  46.7 5.1 collective-permute-start
  55.4 14.9 %all_gather.26 = bf16[256,8,128]{2,0,1:T(8,128)(2,1)S(1)} all-gather(bf16[64,8,128]{2,0,1:T(8,128)(2,1)S(1)} %get-tuple-element.2151), channel_id=1, replica_groups=mesh['groups'=2,'section'=4,'filt'=4] {'filt'}, dimensions={0}, use_global_device_ids=true | all-gather | bytes 655360 | tf_op jit(solution)/shard_map/while/body/eval_jaxpr/all_gather | solution.py:136
  72.6 9.4 copy.273
  86.6 5.8 collective-permute-start
  95.9 13.3 %all_gather.26 = bf16[256,8,128]{2,0,1:T(8,128)(2,1)S(1)} all-gather(bf16[64,8,128]{2,0,1:T(8,128)(2,1)S(1)} %get-tuple-element.2151), channel_id=1, replica_groups=mesh['groups'=2,'section'=4,'filt'=4] {'filt'}, dimensions={0}, use_global_device_ids=true | all-gather | bytes 655360 | tf_op jit(solution)/shard_map/while/body/eval_jaxpr/all_gather | solution.py:136
  111.5 9.4 copy.273
  125.6 6.9 collective-permute-start
  136.1 13.0 %all_gather.26 = bf16[256,8,128]{2,0,1:T(8,128)(2,1)S(1)} all-gather(bf16[64,8,128]{2,0,1:T(8,128)(2,1)S(1)} %get-tuple-element.2151), channel_id=1, replica_groups=mesh['groups'=2,'section'=4,'filt'=4] {'filt'}, dimensions={0}, use_global_device_ids=true | all-gather | bytes 655360 | tf_op jit(solution)/shard_map/while/body/eval_jaxpr/all_gather | solution.py:136
  151.3 9.4 copy.273
  165.4 6.2 collective-permute-start
  175.2 12.9 %all_gather.26 = bf16[256,8,128]{2,0,1:T(8,128)(2,1)S(1)} all-gather(bf16[64,8,128]{2,0,1:T(8,128)(2,1)S(1)} %get-tuple-element.2151), channel_id=1, replica_groups=mesh['groups'=2,'section'=4,'filt'=4] {'filt'}, dimensions={0}, use_global_device_ids=true | all-gather | bytes 655360 | tf_op jit(solution)/shard_map/while/body/eval_jaxpr/all_gather | solution.py:136
  190.3 9.4 copy.273
  204.3 6.6 collective-permute-start
  214.5 12.4 %all_gather.26 = bf16[256,8,128]{2,0,1:T(8,128)(2,1)S(1)} all-gather(bf16[64,8,128]{2,0,1:T(8,128)(2,1)S(1)} %get-tuple-element.2151), channel_id=1, replica_groups=mesh['groups'=2,'section'=4,'filt'=4] {'filt'}, dimensions={0}, use_global_device_ids=true | all-gather | bytes 655360 | tf_op jit(solution)/shard_map/while/body/eval_jaxpr/all_gather | solution.py:136
  229.2 9.4 copy.273
  243.2 6.8 collective-permute-start
  253.6 13.0 %all_gather.26 = bf16[256,8,128]{2,0,1:T(8,128)(2,1)S(1)} all-gather(bf16[64,8,128]{2,0,1:T(8,128)(2,1)S(1)} %get-tuple-element.2151), channel_id=1, replica_groups=mesh['groups'=2,'section'=4,'filt'=4] {'filt'}, dimensions={0}, use_global_device_ids=true | all-gather | bytes 655360 | tf_op jit(solution)/shard_map/while/body/eval_jaxpr/all_gather | solution.py:136
  268.9 9.4 copy.273
  282.9 6.5 collective-permute-start
  293.0 12.6 %all_gather.26 = bf16[256,8,128]{2,0,1:T(8,128)(2,1)S(1)} all-gather(bf16[64,8,128]{2,0,1:T(8,128)(2,1)S(1)} %get-tuple-element.2151), channel_id=1, replica_groups=mesh['groups'=2,'section'=4,'filt'=4] {'filt'}, dimensions={0}, use_global_device_ids=true | all-gather | bytes 655360 | tf_op jit(solution)/shard_map/while/body/eval_jaxpr/all_gather | solution.py:136
  307.8 9.4 copy.273
  321.8 6.6 collective-permute-start
  332.1 12.6 %all_gather.26 = bf16[256,8,128]{2,0,1:T(8,128)(2,1)S(1)} all-gather(bf16[64,8,128]{2,0,1:T(8,128)(2,1)S(1)} %get-tuple-element.2151), channel_id=1, replica_groups=mesh['groups'=2,'section'=4,'filt'=4] {'filt'}, dimensions={0}, use_global_device_ids=true | all-gather | bytes 655360 | tf_op jit(solution)/shard_map/while/body/eval_jaxpr/all_gather | solution.py:136
  346.9 9.4 copy.273
  360.9 6.9 collective-permute-start
  371.4 12.2 %all_gather.26 = bf16[256,8,128]{2,0,1:T(8,128)(2,1)S(1)} all-gather(bf16[64,8,128]{2,0,1:T(8,128)(2,1)S(1)} %get-tuple-element.2151), channel_id=1, replica_groups=mesh['groups'=2,'section'=4,'filt'=4] {'filt'}, dimensions={0}, use_global_device_ids=true | all-gather | bytes 655360 | tf_op jit(solution)/shard_map/while/body/eval_jaxpr/all_gather | solution.py:136
  385.8 9.4 copy.273
  399.9 7.0 collective-permute-start
  410.5 12.2 %all_gather.26 = bf16[256,8,128]{2,0,1:T(8,128)(2,1)S(1)} all-gather(bf16[64,8,128]{2,0,1:T(8,128)(2,1)S(1)} %get-tuple-element.2151), channel_id=1, replica_groups=mesh['groups'=2,'section'=4,'filt'=4] {'filt'}, dimensions={0}, use_global_device_ids=true | all-gather | bytes 655360 | tf_op jit(solution)/shard_map/while/body/eval_jaxpr/all_gather | solution.py:136
  425.0 9.4 copy.273
  439.0 7.2 collective-permute-start
  449.3 596.6 %while.46 = (s32[]{:T(128)}, bf16[64,8,128]{2,1,0:T(8,128)(2,1)S(1)}, f32[1728,256]{1,0:T(8,128)}, f32[64]{0:T(128)}, bf16[8,64,8,128]{3,2,1,0:T(8,128)(2,1)}, /...) while((s32[]{:T(128)}, ...), condition=%wide.region_5.6_spmd.clone.clone.clone, body=%wide.region_2.5_spmd.sunk.clone.clone.clone.sunk | while | flops 1849737728 | bytes 33530844 | solution.py:201
  472.5 18.2 %all-gather.4 = bf16[1,256,8,128]{3,1,2,0:T(8,128)(2,1)S(1)} all-gather(bf16[1,64,8,128]{3,1,2,0:T(8,128)(2,1)} %constant_dynamic-slice_fusion.13), channel_id=2, replica_groups=mesh['groups'=2,'section'=4,'filt'=4] {'filt'}, dimensions={1}, use_global_device_ids=true | all-gather | bytes 655360 | tf_op jit(solution)/shard_map/while/body/eval_jaxpr/all_gather | solution.py:174
  498.0 4.9 collective-permute-done.1
  525.9 20.0 %all-gather.4 = bf16[1,256,8,128]{3,1,2,0:T(8,128)(2,1)S(1)} all-gather(bf16[1,64,8,128]{3,1,2,0:T(8,128)(2,1)} %constant_dynamic-slice_fusion.13), channel_id=2, replica_groups=mesh['groups'=2,'section'=4,'filt'=4] {'filt'}, dimensions={1}, use_global_device_ids=true | all-gather | bytes 655360 | tf_op jit(solution)/shard_map/while/body/eval_jaxpr/all_gather | solution.py:174
  580.5 20.0 %all-gather.4 = bf16[1,256,8,128]{3,1,2,0:T(8,128)(2,1)S(1)} all-gather(bf16[1,64,8,128]{3,1,2,0:T(8,128)(2,1)} %constant_dynamic-slice_fusion.13), channel_id=2, replica_groups=mesh['groups'=2,'section'=4,'filt'=4] {'filt'}, dimensions={1}, use_global_device_ids=true | all-gather | bytes 655360 | tf_op jit(solution)/shard_map/while/body/eval_jaxpr/all_gather | solution.py:174
  635.1 19.3 %all-gather.4 = bf16[1,256,8,128]{3,1,2,0:T(8,128)(2,1)S(1)} all-gather(bf16[1,64,8,128]{3,1,2,0:T(8,128)(2,1)} %constant_dynamic-slice_fusion.13), channel_id=2, replica_groups=mesh['groups'=2,'section'=4,'filt'=4] {'filt'}, dimensions={1}, use_global_device_ids=true | all-gather | bytes 655360 | tf_op jit(solution)/shard_map/while/body/eval_jaxpr/all_gather | solution.py:174
  689.0 20.1 %all-gather.4 = bf16[1,256,8,128]{3,1,2,0:T(8,128)(2,1)S(1)} all-gather(bf16[1,64,8,128]{3,1,2,0:T(8,128)(2,1)} %constant_dynamic-slice_fusion.13), channel_id=2, replica_groups=mesh['groups'=2,'section'=4,'filt'=4] {'filt'}, dimensions={1}, use_global_device_ids=true | all-gather | bytes 655360 | tf_op jit(solution)/shard_map/while/body/eval_jaxpr/all_gather | solution.py:174
  743.7 19.2 %all-gather.4 = bf16[1,256,8,128]{3,1,2,0:T(8,128)(2,1)S(1)} all-gather(bf16[1,64,8,128]{3,1,2,0:T(8,128)(2,1)} %constant_dynamic-slice_fusion.13), channel_id=2, replica_groups=mesh['groups'=2,'section'=4,'filt'=4] {'filt'}, dimensions={1}, use_global_device_ids=true | all-gather | bytes 655360 | tf_op jit(solution)/shard_map/while/body/eval_jaxpr/all_gather | solution.py:174
  797.5 20.0 %all-gather.4 = bf16[1,256,8,128]{3,1,2,0:T(8,128)(2,1)S(1)} all-gather(bf16[1,64,8,128]{3,1,2,0:T(8,128)(2,1)} %constant_dynamic-slice_fusion.13), channel_id=2, replica_groups=mesh['groups'=2,'section'=4,'filt'=4] {'filt'}, dimensions={1}, use_global_device_ids=true | all-gather | bytes 655360 | tf_op jit(solution)/shard_map/while/body/eval_jaxpr/all_gather | solution.py:174
  818.7 3.8 fusion.217
  852.1 19.3 %all-gather.4 = bf16[1,256,8,128]{3,1,2,0:T(8,128)(2,1)S(1)} all-gather(bf16[1,64,8,128]{3,1,2,0:T(8,128)(2,1)} %constant_dynamic-slice_fusion.13), channel_id=2, replica_groups=mesh['groups'=2,'section'=4,'filt'=4] {'filt'}, dimensions={1}, use_global_device_ids=true | all-gather | bytes 655360 | tf_op jit(solution)/shard_map/while/body/eval_jaxpr/all_gather | solution.py:174
  906.0 20.0 %all-gather.4 = bf16[1,256,8,128]{3,1,2,0:T(8,128)(2,1)S(1)} all-gather(bf16[1,64,8,128]{3,1,2,0:T(8,128)(2,1)} %constant_dynamic-slice_fusion.13), channel_id=2, replica_groups=mesh['groups'=2,'section'=4,'filt'=4] {'filt'}, dimensions={1}, use_global_device_ids=true | all-gather | bytes 655360 | tf_op jit(solution)/shard_map/while/body/eval_jaxpr/all_gather | solution.py:174
  960.7 19.2 %all-gather.4 = bf16[1,256,8,128]{3,1,2,0:T(8,128)(2,1)S(1)} all-gather(bf16[1,64,8,128]{3,1,2,0:T(8,128)(2,1)} %constant_dynamic-slice_fusion.13), channel_id=2, replica_groups=mesh['groups'=2,'section'=4,'filt'=4] {'filt'}, dimensions={1}, use_global_device_ids=true | all-gather | bytes 655360 | tf_op jit(solution)/shard_map/while/body/eval_jaxpr/all_gather | solution.py:174
  1014.4 20.0 %all-gather.4 = bf16[1,256,8,128]{3,1,2,0:T(8,128)(2,1)S(1)} all-gather(bf16[1,64,8,128]{3,1,2,0:T(8,128)(2,1)} %constant_dynamic-slice_fusion.13), channel_id=2, replica_groups=mesh['groups'=2,'section'=4,'filt'=4] {'filt'}, dimensions={1}, use_global_device_ids=true | all-gather | bytes 655360 | tf_op jit(solution)/shard_map/while/body/eval_jaxpr/all_gather | solution.py:174
  (796 shorter events, 498.7 us)
Async XLA Ops:
  7.2 3.1 copy-start
  8.9 4.4 copy-start.1
  9.0 4.4 copy-start.2
  9.0 4.4 copy-start.3
  9.0 4.4 copy-start.4
  9.0 4.4 copy-start.6
  46.7 7.0 collective-permute-start
  86.6 7.7 collective-permute-start
  125.6 8.9 collective-permute-start
  165.4 8.2 collective-permute-start
  204.3 8.5 collective-permute-start
  243.2 8.8 collective-permute-start
  282.9 8.4 collective-permute-start
  321.8 8.6 collective-permute-start
  360.9 8.8 collective-permute-start
  399.9 9.0 collective-permute-start
  439.0 9.2 collective-permute-start
  449.4 44.2 %reduce-scatter.2.cloned.1.call-start = ((), (), s32[]{:S(2)}) async-start(), calls=%async_computation.1 | async-start | bytes 655360 | tf_op jit(solution)/shard_map/while/body/eval_jaxpr/reduce_scatter | solution.py:182
  493.6 9.3 collective-permute-start.1
  502.9 48.1 %reduce-scatter.2.cloned.1.call-start = ((), (), s32[]{:S(2)}) async-start(), calls=%async_computation.1 | async-start | bytes 655360 | tf_op jit(solution)/shard_map/while/body/eval_jaxpr/reduce_scatter | solution.py:182
  551.0 6.5 collective-permute-start.1
  557.5 48.1 %reduce-scatter.2.cloned.1.call-start = ((), (), s32[]{:S(2)}) async-start(), calls=%async_computation.1 | async-start | bytes 655360 | tf_op jit(solution)/shard_map/while/body/eval_jaxpr/reduce_scatter | solution.py:182
  605.6 6.5 collective-permute-start.1
  612.1 47.4 %reduce-scatter.2.cloned.1.call-start = ((), (), s32[]{:S(2)}) async-start(), calls=%async_computation.1 | async-start | bytes 655360 | tf_op jit(solution)/shard_map/while/body/eval_jaxpr/reduce_scatter | solution.py:182
  659.5 6.5 collective-permute-start.1
  666.0 48.2 %reduce-scatter.2.cloned.1.call-start = ((), (), s32[]{:S(2)}) async-start(), calls=%async_computation.1 | async-start | bytes 655360 | tf_op jit(solution)/shard_map/while/body/eval_jaxpr/reduce_scatter | solution.py:182
  714.2 6.5 collective-permute-start.1
  720.7 47.3 %reduce-scatter.2.cloned.1.call-start = ((), (), s32[]{:S(2)}) async-start(), calls=%async_computation.1 | async-start | bytes 655360 | tf_op jit(solution)/shard_map/while/body/eval_jaxpr/reduce_scatter | solution.py:182
  767.9 6.5 collective-permute-start.1
  774.4 48.1 %reduce-scatter.2.cloned.1.call-start = ((), (), s32[]{:S(2)}) async-start(), calls=%async_computation.1 | async-start | bytes 655360 | tf_op jit(solution)/shard_map/while/body/eval_jaxpr/reduce_scatter | solution.py:182
  822.6 6.5 collective-permute-start.1
  829.0 47.4 %reduce-scatter.2.cloned.1.call-start = ((), (), s32[]{:S(2)}) async-start(), calls=%async_computation.1 | async-start | bytes 655360 | tf_op jit(solution)/shard_map/while/body/eval_jaxpr/reduce_scatter | solution.py:182
  876.5 6.5 collective-permute-start.1
  883.0 48.1 %reduce-scatter.2.cloned.1.call-start = ((), (), s32[]{:S(2)}) async-start(), calls=%async_computation.1 | async-start | bytes 655360 | tf_op jit(solution)/shard_map/while/body/eval_jaxpr/reduce_scatter | solution.py:182
  931.1 6.5 collective-permute-start.1
  937.6 47.3 %reduce-scatter.2.cloned.1.call-start = ((), (), s32[]{:S(2)}) async-start(), calls=%async_computation.1 | async-start | bytes 655360 | tf_op jit(solution)/shard_map/while/body/eval_jaxpr/reduce_scatter | solution.py:182
  984.9 6.5 collective-permute-start.1
  991.4 48.1 %reduce-scatter.2.cloned.1.call-start = ((), (), s32[]{:S(2)}) async-start(), calls=%async_computation.1 | async-start | bytes 655360 | tf_op jit(solution)/shard_map/while/body/eval_jaxpr/reduce_scatter | solution.py:182
  1039.5 6.5 collective-permute-start.1
  1048.8 3.8 copy-start.5
Sparse Core Ops, SparseCore 0:
  469.5 23.8 reduce-scatter.1
  522.9 23.7 reduce-scatter.1
  577.5 22.9 reduce-scatter.1
  632.1 22.2 reduce-scatter.1
  686.0 23.0 reduce-scatter.1
  740.7 21.9 reduce-scatter.1
  794.5 22.9 reduce-scatter.1
  849.1 22.2 reduce-scatter.1
  903.0 22.9 reduce-scatter.1
  957.7 21.8 reduce-scatter.1
  1011.4 22.9 reduce-scatter.1
where the time goes:
time: 1070 us; the launch traced here: 1060 us
  blocking collectives  360 us (34%)
  local copies, waits for them, and re-layouts  233 us (22%)
  other arithmetic  189 us (18%)
  matrix products  132 us (12%)
  starting transfers between devices  93.6 us (9%)
  waiting for transfers between devices  36.5 us (3%)
  between operations  13.8 us (1%)
    all_gather x11, blocking collectives, backward_tick(): lax.all_gather(for_sending(own_input), 'filt', axis=0, tiled=True)  215 us
    all_gather x11, blocking collectives, forward_tick(): lax.all_gather(a, 'filt', axis=0, tiled=True)  144 us
    while x253, other arithmetic  107 us
    dot_general x11, local copies, waits for them, and re-layouts, forward_tick(): jnp.einsum('ki,irz->krz', columns, panel_part, preferred_element_type=jnp...  104 us
    ppermute x22, starting transfers between devices, passed_along(): lax.ppermute(value, axis, [(source, source + steps) for source in range(f...  93.5 us
    dot_general x11, matrix products, backward_tick(): jnp.einsum('krz,irz->ki', stacked, lax.all_gather(for_sending(own_input),...  40.4 us
    dynamic_slice x33, local copies, waits for them, and re-layouts, store_slot(): previous = lax.dynamic_index_in_dim(buffer, position, 0, keepdims=False)  38 us
    ppermute x22, waiting for transfers between devices, passed_along(): lax.ppermute(value, axis, [(source, source + steps) for source in range(f...  36.3 us
  transfers between devices with their start and end apart: 33, of which 22 were waited for; matrix products, arithmetic and copies ran while one was open for 12% of the time, Pallas kernels for 0%

commit v1 on v0

--- a/solution.py
+++ b/solution.py
@@ -8,6 +8,28 @@
 tap_offsets = [
     (first, second, third) for first in (-1, 0, 1) for second in (-1, 0, 1) for third in (-1, 0, 1)
 ]
+
+
+def laid_out(tiles, dim):
+    tiles = jnp.moveaxis(tiles, 0, dim)
+    lengths = tiles.shape
+    return tiles.reshape(*lengths[:dim], lengths[dim] * lengths[dim + 1], *lengths[dim + 2 :])
+
+
+def gather_around(value, axis, dim):
+    size = lax.axis_size(axis)
+    pairs = [(i, (i + 1) % size) for i in range(size)]
+    back = [(b, a) for a, b in pairs]
+    lower, upper = ([], [])
+    for lap in range(size - 1):
+        if lap % 2 == 0:
+            lower.append(lax.ppermute(lower[-1] if lower else value, axis, pairs))
+        else:
+            upper.append(lax.ppermute(upper[-1] if upper else value, axis, back))
+    blocks = jnp.stack([*lower[::-1], value, *upper])
+    shift = lax.axis_index(axis) - len(lower)
+    blocks = blocks[(jnp.arange(size) - shift) % size]
+    return laid_out(blocks, dim)
 
 
 def passed_along(value, axis, steps):
@@ -132,9 +154,7 @@
         position = jnp.clip(sample, 0, micro_count - 1)
         first_input = lax.dynamic_index_in_dim(flat_volumes, position, 0, keepdims=False)
         own_input = jnp.where(section_pos == 0, first_input, incoming)
-        panel_part = jax.tree.map(
-            lambda a: lax.all_gather(a, "filt", axis=0, tiled=True), own_input
-        )
+        panel_part = jax.tree.map(lambda a: gather_around(a, "filt", 0), own_input)
         columns = lax.slice_in_dim(weight_rows, 0, panel_part.shape[0], axis=1)
         product = jnp.zeros(
             (own_count * tap_count, row_total, lane_count), jnp.float32

time: 1070 us -> 1060 us (level)
  blocking collectives: 360 us -> 203 us
  waiting for transfers between devices: 36.5 us -> 134 us
  starting transfers between devices: 93.6 us -> 130 us
  other arithmetic: 189 us -> 201 us
    all_gather x11 -> x0, blocking collectives: 144 us -> none  [forward_tick(): lax.all_gather(a, 'filt', axis=0, tiled=True)]
    ppermute x0 -> x33, waiting for transfers between devices: none -> 77.9 us  [the longest x22 76.4 us: gather_around(): lower.append(lax.ppermute(lower[-1] if lower else value, axis, pairs))]
    ppermute x0 -> x33, starting transfers between devices: none -> 36.8 us  [the longest x11 34.6 us: gather_around(): upper.append(lax.ppermute(upper[-1] if upper else value, axis, back))]
    ppermute x22, waiting for transfers between devices: 36.3 us -> 56 us  [passed_along(): lax.ppermute(value, axis, [(source, source + steps) for source in range(f...]
    dynamic_slice x11 -> x22, local copies, waits for them, and re-layouts: 17.1 us -> 34.5 us  [backward_tick(): own_input = lax.dynamic_index_in_dim(stored, position, 0, keepdims=False)]
    all_gather x11, blocking collectives: 215 us -> 203 us  [backward_tick(): lax.all_gather(for_sending(own_input), 'filt', axis=0, tiled=True)]
  transfers between devices with their start and end apart: 33 -> 66, of which waited for: 22 -> 45; matrix products, arithmetic and copies ran while one was open for 12% -> 14% of each run, Pallas kernels for 0% -> 0%
where the time goes in v1:
time: 1060 us; the launch traced here: 1050 us
  local copies, waits for them, and re-layouts  232 us (22%)
  blocking collectives  203 us (19%)
  other arithmetic  201 us (19%)
  matrix products  136 us (13%)
  waiting for transfers between devices  134 us (13%)
  starting transfers between devices  130 us (12%)
  between operations  13.8 us (1%)
    all_gather x11, blocking collectives, backward_tick(): lax.all_gather(for_sending(own_input), 'filt', axis=0, tiled=True)  203 us
    while x253, other arithmetic  107 us
    dot_general x11, local copies, waits for them, and re-layouts, forward_tick(): jnp.einsum('ki,irz->krz', columns, panel_part, preferred_element_type=jnp...  104 us
    ppermute x22, starting transfers between devices, passed_along(): lax.ppermute(value, axis, [(source, source + steps) for source in range(f...  93.4 us
    ppermute x22, waiting for transfers between devices, gather_around(): lower.append(lax.ppermute(lower[-1] if lower else value, axis, pairs))  76.4 us
    ppermute x22, waiting for transfers between devices, passed_along(): lax.ppermute(value, axis, [(source, source + steps) for source in range(f...  56 us
    dynamic_update_slice x33, other arithmetic, store_slot(): lax.dynamic_update_index_in_dim(buffer, jnp.where(in_range, entry, previo...  44.3 us
    dot_general x11, matrix products, backward_tick(): jnp.einsum('krz,irz->ki', stacked, lax.all_gather(for_sending(own_input),...  40.4 us
  transfers between devices with their start and end apart: 66, of which 45 were waited for; matrix products, arithmetic and copies ran while one was open for 14% of the time, Pallas kernels for 0%

profile of v1, /device:TPU:1, one launch (start us, length us, event | category | flops | bytes accessed | tf_op | source)
XLA Modules:
  0.0 1051.1 jit_solution(13681950284693477151)
XLA Ops:
  12.8 423.1 %while.45 = (s32[]{:T(128)}, bf16[64,8,128]{2,1,0:T(8,128)(2,1)S(1)}, f32[8,64,8,128]{3,2,1,0:T(8,128)}, bf16[8,64,8,128]{3,2,1,0:T(8,128)(2,1)}, pred[]{:T(512)...) while((s32[]{:T(128)}, ...), condition=%wide.region_1.2_spmd.clone.clone, body=%wide.region_0.1_spmd.sunk.clone.clone.sunk | while | flops 1111983360 | bytes 49661480 | solution.py:174
  31.3 9.4 copy.216
  44.3 6.5 collective-permute-start.3
  62.4 4.6 collective-permute-done.2
  70.0 9.4 copy.216
  83.0 6.1 collective-permute-start.3
  100.2 4.6 collective-permute-done.2
  107.8 9.4 copy.216
  120.8 6.6 collective-permute-start.3
  138.5 4.6 collective-permute-done.2
  146.1 9.4 copy.216
  159.1 6.7 collective-permute-start.3
  176.8 4.6 collective-permute-done.2
  184.4 9.4 copy.216
  197.4 6.6 collective-permute-start.3
  215.1 4.6 collective-permute-done.2
  222.7 9.4 copy.216
  235.7 6.7 collective-permute-start.3
  253.5 4.6 collective-permute-done.2
  261.1 9.4 copy.216
  274.1 6.7 collective-permute-start.3
  291.8 4.6 collective-permute-done.2
  299.4 9.4 copy.216
  312.4 6.7 collective-permute-start.3
  330.1 4.6 collective-permute-done.2
  337.7 9.4 copy.216
  350.7 6.6 collective-permute-start.3
  368.4 4.6 collective-permute-done.2
  376.1 9.4 copy.216
  389.0 6.6 collective-permute-start.3
  406.8 4.6 collective-permute-done.2
  414.4 9.4 copy.216
  427.4 6.6 collective-permute-start.3
  437.1 600.4 %while.46 = (s32[]{:T(128)}, bf16[64,8,128]{2,1,0:T(8,128)(2,1)S(1)}, f32[1728,256]{1,0:T(8,128)}, f32[64]{0:T(128)}, bf16[8,64,8,128]{3,2,1,0:T(8,128)(2,1)}, /...) while((s32[]{:T(128)}, ...), condition=%wide.region_5.6_spmd.clone.clone.clone, body=%wide.region_2.5_spmd.sunk.clone.clone.clone.sunk | while | flops 1849737728 | bytes 33268696 | solution.py:221
  460.9 17.6 %all-gather.4 = bf16[1,256,8,128]{3,1,2,0:T(8,128)(2,1)S(1)} all-gather(bf16[1,64,8,128]{3,1,2,0:T(8,128)(2,1)} %copy.221), channel_id=2, replica_groups=mesh['groups'=2,'section'=4,'filt'=4] {'filt'}, dimensions={1}, use_global_device_ids=true | all-gather | bytes 655360 | tf_op jit(solution)/shard_map/while/body/eval_jaxpr/all_gather | solution.py:194
  485.0 4.9 collective-permute-done.4
  513.6 19.9 %all-gather.4 = bf16[1,256,8,128]{3,1,2,0:T(8,128)(2,1)S(1)} all-gather(bf16[1,64,8,128]{3,1,2,0:T(8,128)(2,1)} %copy.221), channel_id=2, replica_groups=mesh['groups'=2,'section'=4,'filt'=4] {'filt'}, dimensions={1}, use_global_device_ids=true | all-gather | bytes 655360 | tf_op jit(solution)/shard_map/while/body/eval_jaxpr/all_gather | solution.py:194
  568.9 19.2 %all-gather.4 = bf16[1,256,8,128]{3,1,2,0:T(8,128)(2,1)S(1)} all-gather(bf16[1,64,8,128]{3,1,2,0:T(8,128)(2,1)} %copy.221), channel_id=2, replica_groups=mesh['groups'=2,'section'=4,'filt'=4] {'filt'}, dimensions={1}, use_global_device_ids=true | all-gather | bytes 655360 | tf_op jit(solution)/shard_map/while/body/eval_jaxpr/all_gather | solution.py:194
  623.5 19.0 %all-gather.4 = bf16[1,256,8,128]{3,1,2,0:T(8,128)(2,1)S(1)} all-gather(bf16[1,64,8,128]{3,1,2,0:T(8,128)(2,1)} %copy.221), channel_id=2, replica_groups=mesh['groups'=2,'section'=4,'filt'=4] {'filt'}, dimensions={1}, use_global_device_ids=true | all-gather | bytes 655360 | tf_op jit(solution)/shard_map/while/body/eval_jaxpr/all_gather | solution.py:194
  678.4 18.6 %all-gather.4 = bf16[1,256,8,128]{3,1,2,0:T(8,128)(2,1)S(1)} all-gather(bf16[1,64,8,128]{3,1,2,0:T(8,128)(2,1)} %copy.221), channel_id=2, replica_groups=mesh['groups'=2,'section'=4,'filt'=4] {'filt'}, dimensions={1}, use_global_device_ids=true | all-gather | bytes 655360 | tf_op jit(solution)/shard_map/while/body/eval_jaxpr/all_gather | solution.py:194
  733.0 18.5 %all-gather.4 = bf16[1,256,8,128]{3,1,2,0:T(8,128)(2,1)S(1)} all-gather(bf16[1,64,8,128]{3,1,2,0:T(8,128)(2,1)} %copy.221), channel_id=2, replica_groups=mesh['groups'=2,'section'=4,'filt'=4] {'filt'}, dimensions={1}, use_global_device_ids=true | all-gather | bytes 655360 | tf_op jit(solution)/shard_map/while/body/eval_jaxpr/all_gather | solution.py:194
  787.8 18.1 %all-gather.4 = bf16[1,256,8,128]{3,1,2,0:T(8,128)(2,1)S(1)} all-gather(bf16[1,64,8,128]{3,1,2,0:T(8,128)(2,1)} %copy.221), channel_id=2, replica_groups=mesh['groups'=2,'section'=4,'filt'=4] {'filt'}, dimensions={1}, use_global_device_ids=true | all-gather | bytes 655360 | tf_op jit(solution)/shard_map/while/body/eval_jaxpr/all_gather | solution.py:194
  842.4 18.1 %all-gather.4 = bf16[1,256,8,128]{3,1,2,0:T(8,128)(2,1)S(1)} all-gather(bf16[1,64,8,128]{3,1,2,0:T(8,128)(2,1)} %copy.221), channel_id=2, replica_groups=mesh['groups'=2,'section'=4,'filt'=4] {'filt'}, dimensions={1}, use_global_device_ids=true | all-gather | bytes 655360 | tf_op jit(solution)/shard_map/while/body/eval_jaxpr/all_gather | solution.py:194
  897.3 17.8 %all-gather.4 = bf16[1,256,8,128]{3,1,2,0:T(8,128)(2,1)S(1)} all-gather(bf16[1,64,8,128]{3,1,2,0:T(8,128)(2,1)} %copy.221), channel_id=2, replica_groups=mesh['groups'=2,'section'=4,'filt'=4] {'filt'}, dimensions={1}, use_global_device_ids=true | all-gather | bytes 655360 | tf_op jit(solution)/shard_map/while/body/eval_jaxpr/all_gather | solution.py:194
  923.7 4.3 collective-permute-done.4
  951.8 18.1 %all-gather.4 = bf16[1,256,8,128]{3,1,2,0:T(8,128)(2,1)S(1)} all-gather(bf16[1,64,8,128]{3,1,2,0:T(8,128)(2,1)} %copy.221), channel_id=2, replica_groups=mesh['groups'=2,'section'=4,'filt'=4] {'filt'}, dimensions={1}, use_global_device_ids=true | all-gather | bytes 655360 | tf_op jit(solution)/shard_map/while/body/eval_jaxpr/all_gather | solution.py:194
  1006.6 17.8 %all-gather.4 = bf16[1,256,8,128]{3,1,2,0:T(8,128)(2,1)S(1)} all-gather(bf16[1,64,8,128]{3,1,2,0:T(8,128)(2,1)} %copy.221), channel_id=2, replica_groups=mesh['groups'=2,'section'=4,'filt'=4] {'filt'}, dimensions={1}, use_global_device_ids=true | all-gather | bytes 655360 | tf_op jit(solution)/shard_map/while/body/eval_jaxpr/all_gather | solution.py:194
  1033.1 4.4 collective-permute-done.4
  (760 shorter events, 596.3 us)
Async XLA Ops:
  15.4 7.3 collective-permute-start.1
  17.5 7.7 collective-permute-start
  44.3 8.4 collective-permute-start.3
  55.3 6.2 collective-permute-start.1
  55.3 7.1 collective-permute-start
  61.4 5.6 collective-permute-start.2
  83.0 8.1 collective-permute-start.3
  93.6 5.6 collective-permute-start.1
  93.6 6.6 collective-permute-start
  120.8 8.6 collective-permute-start.3
  131.9 6.6 collective-permute-start
  159.1 8.6 collective-permute-start.3
  170.2 6.6 collective-permute-start
  197.4 8.6 collective-permute-start.3
  208.5 6.6 collective-permute-start
  235.7 8.6 collective-permute-start.3
  246.9 6.6 collective-permute-start
  274.1 8.6 collective-permute-start.3
  285.2 6.6 collective-permute-start
  312.4 8.6 collective-permute-start.3
  323.5 6.6 collective-permute-start
  350.7 8.6 collective-permute-start.3
  361.8 6.6 collective-permute-start
  389.0 8.6 collective-permute-start.3
  400.2 6.6 collective-permute-start
  427.4 8.6 collective-permute-start.3
  437.1 44.4 %reduce-scatter.2.cloned.1.call-start = ((), (), s32[]{:S(2)}) async-start(), calls=%async_computation.1 | async-start | bytes 655360 | tf_op jit(solution)/shard_map/while/body/eval_jaxpr/reduce_scatter | solution.py:202
  481.5 8.4 collective-permute-start.4
  489.9 48.7 %reduce-scatter.2.cloned.1.call-start = ((), (), s32[]{:S(2)}) async-start(), calls=%async_computation.1 | async-start | bytes 655360 | tf_op jit(solution)/shard_map/while/body/eval_jaxpr/reduce_scatter | solution.py:202
  538.7 6.5 collective-permute-start.4
  545.1 48.0 %reduce-scatter.2.cloned.1.call-start = ((), (), s32[]{:S(2)}) async-start(), calls=%async_computation.1 | async-start | bytes 655360 | tf_op jit(solution)/shard_map/while/body/eval_jaxpr/reduce_scatter | solution.py:202
  593.1 6.7 collective-permute-start.4
  599.8 47.8 %reduce-scatter.2.cloned.1.call-start = ((), (), s32[]{:S(2)}) async-start(), calls=%async_computation.1 | async-start | bytes 655360 | tf_op jit(solution)/shard_map/while/body/eval_jaxpr/reduce_scatter | solution.py:202
  647.6 7.0 collective-permute-start.4
  654.7 47.5 %reduce-scatter.2.cloned.1.call-start = ((), (), s32[]{:S(2)}) async-start(), calls=%async_computation.1 | async-start | bytes 655360 | tf_op jit(solution)/shard_map/while/body/eval_jaxpr/reduce_scatter | solution.py:202
  702.1 7.1 collective-permute-start.4
  709.2 47.4 %reduce-scatter.2.cloned.1.call-start = ((), (), s32[]{:S(2)}) async-start(), calls=%async_computation.1 | async-start | bytes 655360 | tf_op jit(solution)/shard_map/while/body/eval_jaxpr/reduce_scatter | solution.py:202
  756.6 7.5 collective-permute-start.4
  764.1 47.0 %reduce-scatter.2.cloned.1.call-start = ((), (), s32[]{:S(2)}) async-start(), calls=%async_computation.1 | async-start | bytes 655360 | tf_op jit(solution)/shard_map/while/body/eval_jaxpr/reduce_scatter | solution.py:202
  811.1 7.5 collective-permute-start.4
  818.6 46.9 %reduce-scatter.2.cloned.1.call-start = ((), (), s32[]{:S(2)}) async-start(), calls=%async_computation.1 | async-start | bytes 655360 | tf_op jit(solution)/shard_map/while/body/eval_jaxpr/reduce_scatter | solution.py:202
  865.6 7.9 collective-permute-start.4
  873.5 46.6 %reduce-scatter.2.cloned.1.call-start = ((), (), s32[]{:S(2)}) async-start(), calls=%async_computation.1 | async-start | bytes 655360 | tf_op jit(solution)/shard_map/while/body/eval_jaxpr/reduce_scatter | solution.py:202
  920.1 7.9 collective-permute-start.4
  928.1 46.9 %reduce-scatter.2.cloned.1.call-start = ((), (), s32[]{:S(2)}) async-start(), calls=%async_computation.1 | async-start | bytes 655360 | tf_op jit(solution)/shard_map/while/body/eval_jaxpr/reduce_scatter | solution.py:202
  975.0 7.8 collective-permute-start.4
  982.8 46.7 %reduce-scatter.2.cloned.1.call-start = ((), (), s32[]{:S(2)}) async-start(), calls=%async_computation.1 | async-start | bytes 655360 | tf_op jit(solution)/shard_map/while/body/eval_jaxpr/reduce_scatter | solution.py:202
  1029.5 7.9 collective-permute-start.4
  (24 other events, 132.9 us)
Sparse Core Ops, SparseCore 0:
  456.3 22.3 reduce-scatter.1
  509.1 24.3 reduce-scatter.1
  564.3 23.7 reduce-scatter.1
  619.0 23.5 reduce-scatter.1
  673.8 22.9 reduce-scatter.1
  728.4 22.7 reduce-scatter.1
  783.2 21.7 reduce-scatter.1
  837.8 21.2 reduce-scatter.1
  892.6 20.7 reduce-scatter.1
  947.2 21.2 reduce-scatter.1
  1002.0 20.8 reduce-scatter.1
